TPU v7x, 128 devices: a whole 4x4x4 slice. The times are simulated.
128 devices in a mesh: src: 16 (over y_lo, z, core), tgt: 8 (over y_hi, x).
Axes of the slice: x: 4, y: 4 (y_hi: 2, y_lo: 2; y = y_hi * 2 + y_lo), z: 4, core: 2. Of those that a mesh axis runs over, the one named last changes fastest.
Arguments:
- src_emb: bfloat16 [16384, 768], P(('src', 'tgt')), may hold values from -0.05119037 to 0.05119037
- right_sentence_vectors: bfloat16 [8192, 768], P(('tgt', 'src')), may hold values from -0.05119037 to 0.05119037
- src_mass: float32 [16384], P('src'), may hold values from 0.25 to 4
- tgt_mass: float32 [8192], P('tgt'), may hold values from 0.5 to 8
Outputs:
- grad_src: float32 [16384, 768], P(('src', 'tgt'))
- grad_tgt: float32 [8192, 768], P(('tgt', 'src'))
All inputs are finite; a program needn't handle non-finite values.
Results may differ from a plain program's by a relative error of at most 0.00045.
Values may be sent and summed in bfloat16 or wider, within the bound.
No kernel may reach another device: no remote copies, remote signals or barrier semaphores. Data moves between devices by JAX's collectives and lax.ppermute only.
A program may use at most 64 MiB of HBM per device.

v0:
```python
import jax
import jax.numpy as jnp
from jax import lax
from jax.sharding import PartitionSpec as P

ITERS = 4
regularizer_epsilon = 0.05
highest = lax.Precision.HIGHEST


def row_total(part):
    return lax.psum(part, "tgt")


def col_total(part):
    return lax.psum(part, "src")


def times_vector(kernel, vector):
    return jnp.dot(kernel, vector, precision=highest, preferred_element_type=jnp.float32)


def vector_times(vector, kernel):
    return jnp.dot(vector, kernel, precision=highest, preferred_element_type=jnp.float32)


def per_device(src_emb, right_sentence_vectors, src_mass, tgt_mass):
    src_rows = lax.all_gather(src_emb, "tgt", axis=0, tiled=True)
    target_rows = lax.all_gather(right_sentence_vectors, "src", axis=0, tiled=True)

    def build():
        kernel_grid = (
            lax.dot_general(
                src_rows, target_rows, (((1,), (1,)), ((), ())), preferred_element_type=jnp.float32
            )
            / regularizer_epsilon
        )
        kernel = lax.optimization_barrier(jnp.exp(kernel_grid).astype(jnp.bfloat16))
        return (kernel_grid, kernel)

    kernel_grid, kernel = build()
    vector = jnp.ones(tgt_mass.shape, jnp.float32)
    old_saved, row_saved, src_saved, col_saved, tgt_saved = ([], [], [], [], [])
    for iteration in range(ITERS):
        old_saved.append(vector)
        row_sum = row_total(times_vector(kernel, vector))
        src_scale = src_mass / row_sum
        col_sum = col_total(vector_times(src_scale, kernel))
        vector = tgt_mass / col_sum
        row_saved.append(row_sum)
        src_saved.append(src_scale)
        col_saved.append(col_sum)
        tgt_saved.append(vector)
    last_src = src_saved[-1]
    last_tgt = tgt_saved[-1]
    weighted = kernel * kernel_grid
    src_adj = row_total(times_vector(weighted, last_tgt))
    tgt_adj = col_total(vector_times(last_src, weighted))
    row_bars = [None] * ITERS
    col_bars = [None] * ITERS
    for iteration in reversed(range(ITERS)):
        kernel_grid, kernel = build()
        col_bar = -tgt_adj * tgt_saved[iteration] / col_saved[iteration]
        back = row_total(times_vector(kernel, col_bar))
        if iteration == ITERS - 1:
            back = back + src_adj
        row_bar = -back * src_saved[iteration] / row_saved[iteration]
        if iteration > 0:
            tgt_adj = col_total(vector_times(row_bar, kernel))
        row_bars[iteration] = row_bar
        col_bars[iteration] = col_bar
    left = jnp.stack(row_bars + src_saved, axis=1)
    right = jnp.stack(old_saved + col_bars, axis=1)
    lowrank = lax.dot_general(
        left, right, (((1,), (1,)), ((), ())), precision=highest, preferred_element_type=jnp.float32
    )
    cross_term_grid = (
        kernel * (last_src[:, None] * last_tgt[None, :] * (1.0 + kernel_grid) + lowrank)
    ).astype(jnp.bfloat16)
    left_share_piece = (
        jnp.dot(cross_term_grid, target_rows, preferred_element_type=jnp.float32)
        / regularizer_epsilon
    )
    right_share_piece = (
        lax.dot_general(
            cross_term_grid, src_rows, (((0,), (0,)), ((), ())), preferred_element_type=jnp.float32
        )
        / regularizer_epsilon
    )
    src_whole = lax.psum(left_share_piece, "tgt")
    tgt_whole = lax.psum(right_share_piece, "src")
    src_count = src_emb.shape[0]
    tgt_count = right_sentence_vectors.shape[0]
    grad_src = lax.dynamic_slice_in_dim(src_whole, lax.axis_index("tgt") * src_count, src_count, 0)
    grad_tgt = lax.dynamic_slice_in_dim(tgt_whole, lax.axis_index("src") * tgt_count, tgt_count, 0)
    return (grad_src, grad_tgt)


def solution(mesh):
    placed = (P(("src", "tgt"), None), P(("tgt", "src"), None), P("src"), P("tgt"))
    return jax.shard_map(
        per_device,
        mesh=mesh,
        in_specs=placed,
        out_specs=(P(("src", "tgt"), None), P(("tgt", "src"), None)),
        check_vma=False,
    )
```

profile of v0, /device:TPU:1, one launch (start us, length us, event | category | flops | bytes accessed | tf_op | source)
XLA Modules:
  0.0 730.8 jit_solution(13594640266932629747)
XLA Ops:
  8.7 54.5 %all-gather.3.cloned.1.call-done = bf16[1024,768]{1,0:T(8,128)(2,1)} async-done(((bf16[128,768]{1,0:T(8,128)(2,1)}), bf16[1024,768]{1,0:T(8,128)(2,1)}) %all-gather.3.cloned.1.call-update) | async-done | bytes 1572880 | tf_op jit(solution)/shard_map/all_gather | solution.py:28
  63.2 35.8 %all-gather.5.cloned.1.call-done = bf16[1024,768]{1,0:T(8,128)(2,1)} async-done(((bf16[64,768]{1,0:T(8,128)(2,1)}), bf16[1024,768]{1,0:T(8,128)(2,1)}) %all-gather.5.cloned.1.call-update) | async-done | bytes 1572880 | tf_op jit(solution)/shard_map/all_gather | solution.py:29
  99.0 5.6 exponential_convert_fusion
  106.4 20.2 %psum.133 = f32[1024]{0:T(1024)S(1)} all-reduce(f32[1024]{0:T(1024)S(1)} %bitcast.122), channel_id=1, replica_groups=mesh['src'=16,'tgt'=8] {'tgt'}, use_global_device_ids=true, to_apply=%region_0.0 | all-reduce | flops 1024 | bytes 8192 | tf_op jit(solution)/shard_map/psum | solution.py:12
  127.5 30.5 %psum.134 = f32[1024]{0:T(1024)S(1)} all-reduce(f32[1024]{0:T(1024)S(1)} %bitcast.123), channel_id=1, replica_groups=mesh['src'=16,'tgt'=8] {'src'}, use_global_device_ids=true, to_apply=%region_1.0 | all-reduce | flops 1024 | bytes 8192 | tf_op jit(solution)/shard_map/psum | solution.py:16
  159.7 15.5 %psum.135 = f32[1024]{0:T(1024)S(1)} all-reduce(f32[1024]{0:T(1024)S(1)} %bitcast.124), channel_id=1, replica_groups=mesh['src'=16,'tgt'=8] {'tgt'}, use_global_device_ids=true, to_apply=%region_2.0 | all-reduce | flops 1024 | bytes 8192 | tf_op jit(solution)/shard_map/psum | solution.py:12
  176.2 30.6 %psum.136 = f32[1024]{0:T(1024)S(1)} all-reduce(f32[1024]{0:T(1024)S(1)} %bitcast.125), channel_id=1, replica_groups=mesh['src'=16,'tgt'=8] {'src'}, use_global_device_ids=true, to_apply=%region_3.0 | all-reduce | flops 1024 | bytes 8192 | tf_op jit(solution)/shard_map/psum | solution.py:16
  206.8 1.7 fusion.13
  208.5 17.2 %psum.137 = f32[1024]{0:T(1024)S(1)} all-reduce(f32[1024]{0:T(1024)S(1)} %bitcast.126), channel_id=1, replica_groups=mesh['src'=16,'tgt'=8] {'tgt'}, use_global_device_ids=true, to_apply=%region_4.0 | all-reduce | flops 1024 | bytes 8192 | tf_op jit(solution)/shard_map/psum | solution.py:12
  226.6 30.9 %psum.138 = f32[1024]{0:T(1024)S(1)} all-reduce(f32[1024]{0:T(1024)S(1)} %bitcast.127), channel_id=1, replica_groups=mesh['src'=16,'tgt'=8] {'src'}, use_global_device_ids=true, to_apply=%region_5.0 | all-reduce | flops 1024 | bytes 8192 | tf_op jit(solution)/shard_map/psum | solution.py:16
  257.5 1.7 fusion.15
  259.3 15.6 %psum.139 = f32[1024]{0:T(1024)S(1)} all-reduce(f32[1024]{0:T(1024)S(1)} %bitcast.128), channel_id=1, replica_groups=mesh['src'=16,'tgt'=8] {'tgt'}, use_global_device_ids=true, to_apply=%region_6.0 | all-reduce | flops 1024 | bytes 8192 | tf_op jit(solution)/shard_map/psum | solution.py:12
  275.8 4.6 fusion.2
  280.5 31.1 %all-reduce = (f32[1024]{0:T(1024)S(1)}, f32[1024]{0:T(1024)S(1)}) all-reduce(f32[1024]{0:T(1024)S(1)} %bitcast.120, f32[1024]{0:T(1024)S(1)} %bitcast.121), channel_id=1, replica_groups=mesh['src'=16,'tgt'=8] {'src'}, use_global_device_ids=true, to_apply=%region_7.0 | all-reduce | flops 2048 | bytes 16384 | tf_op jit(solution)/shard_map/psum | solution.py:16
  311.6 6.1 fusion.1
  317.7 1.7 fusion.17
  319.4 17.2 %psum.152 = f32[1024]{0:T(1024)S(1)} all-reduce(f32[1024]{0:T(1024)S(1)} %add.58), channel_id=1, replica_groups=mesh['src'=16,'tgt'=8] {'tgt'}, use_global_device_ids=true, to_apply=%region_9.0 | all-reduce | flops 1024 | bytes 8192 | tf_op jit(solution)/shard_map/psum | solution.py:12
  337.6 30.9 %psum.144 = f32[1024]{0:T(1024)S(1)} all-reduce(f32[1024]{0:T(1024)S(1)} %bitcast.129), channel_id=1, replica_groups=mesh['src'=16,'tgt'=8] {'src'}, use_global_device_ids=true, to_apply=%region_11.0 | all-reduce | flops 1024 | bytes 8192 | tf_op jit(solution)/shard_map/psum | solution.py:16
  368.5 1.7 fusion.19
  370.2 15.5 %psum.145 = f32[1024]{0:T(1024)S(1)} all-reduce(f32[1024]{0:T(1024)S(1)} %bitcast.130), channel_id=1, replica_groups=mesh['src'=16,'tgt'=8] {'tgt'}, use_global_device_ids=true, to_apply=%region_12.0 | all-reduce | flops 1024 | bytes 8192 | tf_op jit(solution)/shard_map/psum | solution.py:12
  386.7 30.6 %psum.146 = f32[1024]{0:T(1024)S(1)} all-reduce(f32[1024]{0:T(1024)S(1)} %bitcast.131), channel_id=1, replica_groups=mesh['src'=16,'tgt'=8] {'src'}, use_global_device_ids=true, to_apply=%region_13.0 | all-reduce | flops 1024 | bytes 8192 | tf_op jit(solution)/shard_map/psum | solution.py:16
  417.3 1.7 fusion.21
  419.0 17.4 %psum.147 = f32[1024]{0:T(1024)S(1)} all-reduce(f32[1024]{0:T(1024)S(1)} %bitcast.132), channel_id=1, replica_groups=mesh['src'=16,'tgt'=8] {'tgt'}, use_global_device_ids=true, to_apply=%region_14.0 | all-reduce | flops 1024 | bytes 8192 | tf_op jit(solution)/shard_map/psum | solution.py:12
  437.4 30.9 %psum.148 = f32[1024]{0:T(1024)S(1)} all-reduce(f32[1024]{0:T(1024)S(1)} %bitcast.133), channel_id=1, replica_groups=mesh['src'=16,'tgt'=8] {'src'}, use_global_device_ids=true, to_apply=%region_15.0 | all-reduce | flops 1024 | bytes 8192 | tf_op jit(solution)/shard_map/psum | solution.py:16
  468.3 1.7 fusion.23
  470.1 15.5 %psum.149 = f32[1024]{0:T(1024)S(1)} all-reduce(f32[1024]{0:T(1024)S(1)} %bitcast.119), channel_id=1, replica_groups=mesh['src'=16,'tgt'=8] {'tgt'}, use_global_device_ids=true, to_apply=%region_16.0 | all-reduce | flops 1024 | bytes 8192 | tf_op jit(solution)/shard_map/psum | solution.py:12
  485.7 6.2 fusion
  493.2 3.5 convolution_multiply_fusion.1
  498.3 5.0 convolution_multiply_fusion
  503.3 88.4 %all-reduce.4.cloned.1.call-done = f32[1024,768]{1,0:T(8,128)} async-done(((f32[1024,768]{1,0:T(8,128)}), f32[1024,768]{1,0:T(8,128)}) %all-reduce.4.cloned.1.call-update) | async-done | bytes 3145744 | tf_op jit(solution)/shard_map/psum | solution.py:90
  591.8 1.8 constant_dynamic-slice_fusion.1
  593.5 129.1 %all-reduce.6.cloned.1.call-done = f32[1024,768]{1,0:T(8,128)} async-done(((f32[1024,768]{1,0:T(8,128)}), f32[1024,768]{1,0:T(8,128)}) %all-reduce.6.cloned.1.call-update) | async-done | bytes 3145744 | tf_op jit(solution)/shard_map/psum | solution.py:91
  (47 shorter events, 16.2 us)
Async XLA Ops:
  7.2 56.0 %all-gather.3.cloned.1.call-start = ((), (), s32[]{:S(2)}) async-start(), calls=%async_computation | async-start | bytes 1769472 | tf_op jit(solution)/shard_map/all_gather | solution.py:28
  7.9 91.1 %all-gather.5.cloned.1.call-start = ((), (), s32[]{:S(2)}) async-start(), calls=%async_computation.1 | async-start | bytes 1671168 | tf_op jit(solution)/shard_map/all_gather | solution.py:29
  8.6 583.1 %all-reduce.4.cloned.1.call-start = ((), (), s32[]{:S(2)}) async-start(), calls=%async_computation.2 | async-start | bytes 6291456 | tf_op jit(solution)/shard_map/psum | solution.py:90
  104.6 21.9 %copy-start.2 = (f32[1024]{0:T(1024)S(1)}, f32[1024]{0:T(1024)}, u32[]{:S(2)}) copy-start(f32[1024]{0:T(1024)} %param.6) | copy-start | bytes 12292
  104.6 53.4 %copy-start.3 = (f32[1024]{0:T(1024)S(1)}, f32[1024]{0:T(1024)}, u32[]{:S(2)}) copy-start(f32[1024]{0:T(1024)} %param.7) | copy-start | bytes 12292
  485.6 7.6 %copy-start.4 = (bf16[1024,768]{1,0:T(8,128)(2,1)S(1)}, bf16[1024,768]{1,0:T(8,128)(2,1)}, u32[]{:S(2)}) copy-start(bf16[1024,768]{1,0:T(8,128)(2,1)} %all-gather.5.cloned.1.call-done) | copy-start | bytes 4718596
  491.9 1.3 copy-start
  496.7 1.6 copy-start.1
  496.8 225.9 %all-reduce.6.cloned.1.call-start = ((), (), s32[]{:S(2)}) async-start(), calls=%async_computation.3 | async-start | bytes 6291456 | tf_op jit(solution)/shard_map/psum | solution.py:91
Sparse Core Ops, SparseCore 0:
  10.3 52.8 all-gather.2
  64.9 34.0 all-gather.4
  496.9 94.8 all-reduce.3
  594.1 128.4 all-reduce.5
where the time goes:
time: 731 us
  blocking collectives  350 us (48%)
  waiting for transfers between devices  309 us (42%)
  matrix products  51.4 us (7%)
  between operations  13.9 us (2%)
    psum x7, blocking collectives, col_total(): return lax.psum(part, 'src')  216 us
    psum x8, blocking collectives, row_total(): return lax.psum(part, 'tgt')  134 us
    psum x1, waiting for transfers between devices, per_device(): tgt_whole = lax.psum(right_share_piece, 'src')  129 us
    psum x1, waiting for transfers between devices, per_device(): src_whole = lax.psum(left_share_piece, 'tgt')  88.4 us
    all_gather x1, waiting for transfers between devices, per_device(): src_rows = lax.all_gather(src_emb, 'tgt', axis=0, tiled=True)  54.5 us
    all_gather x1, waiting for transfers between devices, per_device(): lax.all_gather(right_sentence_vectors, 'src', axis=0, tiled=True)  35.8 us
    dot_general x9, matrix products, times_vector(): jnp.dot(kernel, vector, precision=highest, preferred_element_type=jnp.flo...  19.9 us
  transfers between devices with their start and end apart: 4, of which 4 were waited for; matrix products, arithmetic and copies ran while one was open for 1% of the time, Pallas kernels for 0%

commit v1 on v0

--- a/solution.py
+++ b/solution.py
@@ -26,7 +26,15 @@
 
 def per_device(src_emb, right_sentence_vectors, src_mass, tgt_mass):
     src_rows = lax.all_gather(src_emb, "tgt", axis=0, tiled=True)
-    target_rows = lax.all_gather(right_sentence_vectors, "src", axis=0, tiled=True)
+    target_rows = jnp.concatenate(
+        lax.all_to_all(
+            jnp.stack([right_sentence_vectors] * lax.axis_size("src"), 0),
+            "src",
+            concat_axis=0,
+            split_axis=0,
+        ),
+        0,
+    )
 
     def build():
         kernel_grid = (

time: 731 us -> 698 us (0.955)
  waiting for transfers between devices: 309 us -> 245 us
  blocking collectives: 350 us -> 380 us
    all_gather x1 -> x0, waiting for transfers between devices: 35.8 us -> none  [per_device(): lax.all_gather(right_sentence_vectors, 'src', axis=0, tiled=True)]
    all_to_all x0 -> x1, blocking collectives: none -> 30.9 us  [per_device(): lax.all_to_all(jnp.stack([right_sentence_vectors] * lax.axis_size('src'),...]
    all_gather x1, waiting for transfers between devices: 54.5 us -> 24.8 us  [per_device(): src_rows = lax.all_gather(src_emb, 'tgt', axis=0, tiled=True)]
  transfers between devices with their start and end apart: 4 -> 3, of which waited for: 4 -> 3; matrix products, arithmetic and copies ran while one was open for 1% -> 1% of each run, Pallas kernels for 0% -> 0%
where the time goes in v1:
time: 698 us
  blocking collectives  380 us (54%)
  waiting for transfers between devices  245 us (35%)
  matrix products  51.4 us (7%)
  between operations  13.9 us (2%)
  local copies, waits for them, and re-layouts  7.43 us (1%)
    psum x7, blocking collectives, col_total(): return lax.psum(part, 'src')  217 us
    psum x8, blocking collectives, row_total(): return lax.psum(part, 'tgt')  132 us
    psum x1, waiting for transfers between devices, per_device(): tgt_whole = lax.psum(right_share_piece, 'src')  129 us
    psum x1, waiting for transfers between devices, per_device(): src_whole = lax.psum(left_share_piece, 'tgt')  90.1 us
    all_to_all x1, blocking collectives, per_device(): lax.all_to_all(jnp.stack([right_sentence_vectors] * lax.axis_size('src'),...  30.9 us
    all_gather x1, waiting for transfers between devices, per_device(): src_rows = lax.all_gather(src_emb, 'tgt', axis=0, tiled=True)  24.8 us
    dot_general x9, matrix products, times_vector(): jnp.dot(kernel, vector, precision=highest, preferred_element_type=jnp.flo...  19.9 us
  transfers between devices with their start and end apart: 3, of which 3 were waited for; matrix products, arithmetic and copies ran while one was open for 1% of the time, Pallas kernels for 0%

profile of v1, /device:TPU:1, one launch (start us, length us, event | category | flops | bytes accessed | tf_op | source)
XLA Modules:
  0.0 697.6 jit_solution(11985994724924811937)
XLA Ops:
  9.0 30.9 %all_to_all.5 = bf16[16,64,768]{2,1,0:T(8,128)(2,1)} all-to-all(bf16[16,64,768]{2,1,0:T(8,128)(2,1)S(1)} %stack.68), channel_id=1, replica_groups=mesh['src'=16,'tgt'=8] {'src'}, dimensions={0} | all-to-all | bytes 3145728 | tf_op jit(solution)/shard_map/all_to_all | solution.py:30
  39.9 24.8 %all-gather.2.cloned.1.call-done = bf16[1024,768]{1,0:T(8,128)(2,1)} async-done(((bf16[128,768]{1,0:T(8,128)(2,1)}), bf16[1024,768]{1,0:T(8,128)(2,1)}) %all-gather.2.cloned.1.call-update) | async-done | bytes 1572880 | tf_op jit(solution)/shard_map/all_gather | solution.py:28
  64.6 5.7 exponential_convert_fusion
  72.0 17.6 %psum.133 = f32[1024]{0:T(1024)S(1)} all-reduce(f32[1024]{0:T(1024)S(1)} %bitcast.125), channel_id=1, replica_groups=mesh['src'=16,'tgt'=8] {'tgt'}, use_global_device_ids=true, to_apply=%region_0.0 | all-reduce | flops 1024 | bytes 8192 | tf_op jit(solution)/shard_map/psum | solution.py:12
  90.6 32.6 %psum.134 = f32[1024]{0:T(1024)S(1)} all-reduce(f32[1024]{0:T(1024)S(1)} %bitcast.126), channel_id=1, replica_groups=mesh['src'=16,'tgt'=8] {'src'}, use_global_device_ids=true, to_apply=%region_1.0 | all-reduce | flops 1024 | bytes 8192 | tf_op jit(solution)/shard_map/psum | solution.py:16
  124.9 15.7 %psum.135 = f32[1024]{0:T(1024)S(1)} all-reduce(f32[1024]{0:T(1024)S(1)} %bitcast.127), channel_id=1, replica_groups=mesh['src'=16,'tgt'=8] {'tgt'}, use_global_device_ids=true, to_apply=%region_2.0 | all-reduce | flops 1024 | bytes 8192 | tf_op jit(solution)/shard_map/psum | solution.py:12
  141.5 30.2 %psum.136 = f32[1024]{0:T(1024)S(1)} all-reduce(f32[1024]{0:T(1024)S(1)} %bitcast.128), channel_id=1, replica_groups=mesh['src'=16,'tgt'=8] {'src'}, use_global_device_ids=true, to_apply=%region_3.0 | all-reduce | flops 1024 | bytes 8192 | tf_op jit(solution)/shard_map/psum | solution.py:16
  171.8 1.7 fusion.13
  173.5 17.2 %psum.137 = f32[1024]{0:T(1024)S(1)} all-reduce(f32[1024]{0:T(1024)S(1)} %bitcast.129), channel_id=1, replica_groups=mesh['src'=16,'tgt'=8] {'tgt'}, use_global_device_ids=true, to_apply=%region_4.0 | all-reduce | flops 1024 | bytes 8192 | tf_op jit(solution)/shard_map/psum | solution.py:12
  191.6 30.9 %psum.138 = f32[1024]{0:T(1024)S(1)} all-reduce(f32[1024]{0:T(1024)S(1)} %bitcast.130), channel_id=1, replica_groups=mesh['src'=16,'tgt'=8] {'src'}, use_global_device_ids=true, to_apply=%region_5.0 | all-reduce | flops 1024 | bytes 8192 | tf_op jit(solution)/shard_map/psum | solution.py:16
  222.5 1.7 fusion.15
  224.2 15.6 %psum.139 = f32[1024]{0:T(1024)S(1)} all-reduce(f32[1024]{0:T(1024)S(1)} %bitcast.131), channel_id=1, replica_groups=mesh['src'=16,'tgt'=8] {'tgt'}, use_global_device_ids=true, to_apply=%region_6.0 | all-reduce | flops 1024 | bytes 8192 | tf_op jit(solution)/shard_map/psum | solution.py:12
  240.8 4.6 fusion.2
  245.4 31.1 %all-reduce = (f32[1024]{0:T(1024)S(1)}, f32[1024]{0:T(1024)S(1)}) all-reduce(f32[1024]{0:T(1024)S(1)} %bitcast.123, f32[1024]{0:T(1024)S(1)} %bitcast.124), channel_id=1, replica_groups=mesh['src'=16,'tgt'=8] {'src'}, use_global_device_ids=true, to_apply=%region_7.0 | all-reduce | flops 2048 | bytes 16384 | tf_op jit(solution)/shard_map/psum | solution.py:16
  276.5 6.1 fusion.1
  282.7 1.7 fusion.17
  284.4 17.2 %psum.152 = f32[1024]{0:T(1024)S(1)} all-reduce(f32[1024]{0:T(1024)S(1)} %add.58), channel_id=1, replica_groups=mesh['src'=16,'tgt'=8] {'tgt'}, use_global_device_ids=true, to_apply=%region_9.0 | all-reduce | flops 1024 | bytes 8192 | tf_op jit(solution)/shard_map/psum | solution.py:12
  302.6 30.9 %psum.144 = f32[1024]{0:T(1024)S(1)} all-reduce(f32[1024]{0:T(1024)S(1)} %bitcast.132), channel_id=1, replica_groups=mesh['src'=16,'tgt'=8] {'src'}, use_global_device_ids=true, to_apply=%region_11.0 | all-reduce | flops 1024 | bytes 8192 | tf_op jit(solution)/shard_map/psum | solution.py:16
  333.5 1.7 fusion.19
  335.2 15.5 %psum.145 = f32[1024]{0:T(1024)S(1)} all-reduce(f32[1024]{0:T(1024)S(1)} %bitcast.133), channel_id=1, replica_groups=mesh['src'=16,'tgt'=8] {'tgt'}, use_global_device_ids=true, to_apply=%region_12.0 | all-reduce | flops 1024 | bytes 8192 | tf_op jit(solution)/shard_map/psum | solution.py:12
  351.7 30.6 %psum.146 = f32[1024]{0:T(1024)S(1)} all-reduce(f32[1024]{0:T(1024)S(1)} %bitcast.134), channel_id=1, replica_groups=mesh['src'=16,'tgt'=8] {'src'}, use_global_device_ids=true, to_apply=%region_13.0 | all-reduce | flops 1024 | bytes 8192 | tf_op jit(solution)/shard_map/psum | solution.py:16
  382.3 1.7 fusion.21
  384.0 17.4 %psum.147 = f32[1024]{0:T(1024)S(1)} all-reduce(f32[1024]{0:T(1024)S(1)} %bitcast.135), channel_id=1, replica_groups=mesh['src'=16,'tgt'=8] {'tgt'}, use_global_device_ids=true, to_apply=%region_14.0 | all-reduce | flops 1024 | bytes 8192 | tf_op jit(solution)/shard_map/psum | solution.py:12
  402.4 30.9 %psum.148 = f32[1024]{0:T(1024)S(1)} all-reduce(f32[1024]{0:T(1024)S(1)} %bitcast.136), channel_id=1, replica_groups=mesh['src'=16,'tgt'=8] {'src'}, use_global_device_ids=true, to_apply=%region_15.0 | all-reduce | flops 1024 | bytes 8192 | tf_op jit(solution)/shard_map/psum | solution.py:16
  433.3 1.7 fusion.23
  435.1 15.5 %psum.149 = f32[1024]{0:T(1024)S(1)} all-reduce(f32[1024]{0:T(1024)S(1)} %bitcast.122), channel_id=1, replica_groups=mesh['src'=16,'tgt'=8] {'tgt'}, use_global_device_ids=true, to_apply=%region_16.0 | all-reduce | flops 1024 | bytes 8192 | tf_op jit(solution)/shard_map/psum | solution.py:12
  450.6 6.2 fusion
  458.2 3.5 convolution_multiply_fusion.1
  463.3 5.0 convolution_multiply_fusion
  468.3 90.1 %all-reduce.4.cloned.1.call-done = f32[1024,768]{1,0:T(8,128)} async-done(((f32[1024,768]{1,0:T(8,128)}), f32[1024,768]{1,0:T(8,128)}) %all-reduce.4.cloned.1.call-update) | async-done | bytes 3145744 | tf_op jit(solution)/shard_map/psum | solution.py:98
  558.5 1.8 constant_dynamic-slice_fusion.1
  560.2 129.2 %all-reduce.6.cloned.1.call-done = f32[1024,768]{1,0:T(8,128)} async-done(((f32[1024,768]{1,0:T(8,128)}), f32[1024,768]{1,0:T(8,128)}) %all-reduce.6.cloned.1.call-update) | async-done | bytes 3145744 | tf_op jit(solution)/shard_map/psum | solution.py:99
  (46 shorter events, 16.5 us)
Async XLA Ops:
  7.2 57.5 %all-gather.2.cloned.1.call-start = ((), (), s32[]{:S(2)}) async-start(), calls=%async_computation.1 | async-start | bytes 1769472 | tf_op jit(solution)/shard_map/all_gather | solution.py:28
  7.9 550.6 %all-reduce.4.cloned.1.call-start = ((), (), s32[]{:S(2)}) async-start(), calls=%async_computation.2 | async-start | bytes 6291456 | tf_op jit(solution)/shard_map/psum | solution.py:98
  70.3 19.3 %copy-start.3 = (f32[1024]{0:T(1024)S(1)}, f32[1024]{0:T(1024)}, u32[]{:S(2)}) copy-start(f32[1024]{0:T(1024)} %param.6) | copy-start | bytes 12292
  70.3 52.8 %copy-start.4 = (f32[1024]{0:T(1024)S(1)}, f32[1024]{0:T(1024)}, u32[]{:S(2)}) copy-start(f32[1024]{0:T(1024)} %param.7) | copy-start | bytes 12292
  450.6 7.6 %copy-start.2 = (bf16[16,64,768]{2,1,0:T(8,128)(2,1)S(1)}, bf16[16,64,768]{2,1,0:T(8,128)(2,1)}, u32[]{:S(2)}) copy-start(bf16[16,64,768]{2,1,0:T(8,128)(2,1)} %all_to_all.5) | copy-start | bytes 4718596
  456.9 1.3 copy-start
  461.7 1.6 copy-start.1
  461.8 227.7 %all-reduce.6.cloned.1.call-start = ((), (), s32[]{:S(2)}) async-start(), calls=%async_computation.3 | async-start | bytes 6291456 | tf_op jit(solution)/shard_map/psum | solution.py:99
Sparse Core Ops, SparseCore 0:
  10.3 54.2 all-gather.1
  461.9 96.5 all-reduce.3
  561.0 128.4 all-reduce.5
